TPU v7x, 512 devices: a whole 4x4x16 slice. The times are simulated.
512 devices in a mesh: seq: 128 (over y, z, core), tp: 4 (over x).
Axes of the slice: x: 4, y: 4, z: 16, core: 2. Of those that a mesh axis runs over, the one named last changes fastest.
Arguments:
- tokens: bfloat16 [32768, 1280], P('seq'), may hold values from -45 to 45
- ln_gain: float32 [1280], replicated, may hold values from 0.6 to 10, as said below
- ln_bias: float32 [1280], replicated, may hold values from -3 to 3
- w_qkv: bfloat16 [3, 1280, 1280], P(None, None, 'tp'), may hold values from -0.15625 to 0.15625
- b_qkv: float32 [3, 1280], P(None, 'tp'), may hold values from -3 to 3
- w_out: bfloat16 [1280, 1280], P('tp'), may hold values from -0.15625 to 0.15625
- b_out: float32 [1280], replicated, may hold values from -3 to 3
- merge_gain: float32 [1280], replicated, may hold values from 0.25 to 1.75
- merge_bias: float32 [1280], replicated, may hold values from -3 to 3
- segments: int32 [8192], replicated, may hold values from 0 to 63, never falling along the last dimension, each value on 1 to 256 neighbouring positions
- owners: int32 [8192, 1], P('seq'), may hold values from 0 to 127; in each aligned block of 64 rows (0 to 63, 64 to 127, ...) at most 2 rows name the same one
Outputs:
- routed: bfloat16 [32768, 5120], P('seq', 'tp')
Inputs may be any that keep to these rules, and one draw needn't show every extreme that they name: `segments`: Non-decreasing along the rows; one image holds at most 256 merged rows, and some image holds exactly that many. `owners`: among the 64 merged rows of one device no owner is named more than 2 times, a bound that some block reaches. `ln_gain`: gains are positive, within 0.6 to 10.
All inputs are finite; a program needn't handle non-finite values.
Results may differ from a plain program's by a relative error of at most 0.024.
The roundings to bfloat16 on the way count: a program that leaves them out, or rounds other values in their place, can miss the bound.
Values may be sent and summed in bfloat16 or wider, within the bound.
No kernel may reach another device: no remote copies, remote signals or barrier semaphores. Data moves between devices by JAX's collectives and lax.ppermute only.
A program may use at most 64 MiB of HBM per device.

v0:
```python
import jax
import jax.numpy as jnp
from jax import lax
from jax.sharding import PartitionSpec as P

HEAD_DIM = 80
SPAN = 4
epsilon = 1e-06
masked_score = -1e30


def from_behind(value, axis, steps):
    count = lax.axis_size(axis)
    leading, last = (max(0, -steps), min(count, count - steps))
    return lax.ppermute(value, axis, [(source, source + steps) for source in range(leading, last)])


def layer_norm(values, gain_row, shift_row):
    center = jnp.mean(values, axis=-1, keepdims=True)
    centered = values - center
    spread = jnp.mean(centered * centered, axis=-1, keepdims=True)
    return centered * lax.rsqrt(spread + epsilon) * gain_row + shift_row


def per_device(
    tokens, ln_gain, ln_bias, w_qkv, b_qkv, w_out, b_out, merge_gain, merge_bias, segments, owners
):
    tok_dev = tokens.shape[0]
    model_width = tokens.shape[1]
    local_width = w_qkv.shape[2]
    local_heads = local_width // HEAD_DIM
    seq_count = lax.axis_size("seq")
    seq_index = lax.axis_index("seq")
    row_start = seq_index * tok_dev
    reach_rows = SPAN * tok_dev
    scale_factor = HEAD_DIM ** (-0.5)
    normed = layer_norm(tokens.astype(jnp.float32), ln_gain, ln_bias).astype(jnp.bfloat16)
    query = (jnp.dot(normed, w_qkv[0], preferred_element_type=jnp.float32) + b_qkv[0]).astype(
        jnp.bfloat16
    )
    key_rows = (jnp.dot(normed, w_qkv[1], preferred_element_type=jnp.float32) + b_qkv[1]).astype(
        jnp.bfloat16
    )
    value_rows = (jnp.dot(normed, w_qkv[2], preferred_element_type=jnp.float32) + b_qkv[2]).astype(
        jnp.bfloat16
    )
    key_value = jnp.concatenate([key_rows, value_rows], axis=1)
    token_segment = jnp.repeat(segments, 4)
    padding = jnp.full((reach_rows,), -1, jnp.int32)
    padded_segment = jnp.concatenate([padding, token_segment, padding])
    query_segment = lax.dynamic_slice_in_dim(token_segment, row_start, tok_dev)
    query_heads = query.reshape(tok_dev, local_heads, HEAD_DIM)

    def segment_window(key_start, length):
        return lax.dynamic_slice_in_dim(padded_segment, key_start + reach_rows, length)

    def block_scores(block, key_segment):
        key_heads = block[:, :local_width].reshape(-1, local_heads, HEAD_DIM)
        value_heads = block[:, local_width:].reshape(-1, local_heads, HEAD_DIM)
        scores = (
            jnp.einsum("qhd,khd->hqk", query_heads, key_heads, preferred_element_type=jnp.float32)
            * scale_factor
        )
        allowed = query_segment[:, None] == key_segment[None, :]
        return (jnp.where(allowed[None], scores, masked_score), value_heads)

    def absorb(state, block, key_segment):
        row_top, totals, summed = state
        scores, value_heads = block_scores(block, key_segment)
        new_top = jnp.maximum(row_top, jnp.max(scores, axis=-1, keepdims=True))
        factor = jnp.exp(row_top - new_top)
        weights = jnp.exp(scores - new_top)
        totals = totals * factor + jnp.sum(weights, axis=-1, keepdims=True)
        summed = summed * factor + jnp.einsum(
            "hqk,khd->hqd",
            weights.astype(jnp.bfloat16),
            value_heads,
            preferred_element_type=jnp.float32,
        )
        return (new_top, totals, summed)

    def absorb_remote(state, block, key_start):
        key_segment = segment_window(key_start, tok_dev)
        return absorb(state, block, key_segment)

    start_state = (
        jnp.full((local_heads, tok_dev, 1), masked_score, jnp.float32),
        jnp.zeros((local_heads, tok_dev, 1), jnp.float32),
        jnp.zeros((local_heads, tok_dev, HEAD_DIM), jnp.float32),
    )
    state = absorb(start_state, key_value, query_segment)
    below = key_value
    above = key_value
    for distance in range(1, SPAN + 1):
        below = from_behind(below, "seq", 1)
        above = from_behind(above, "seq", -1)
        state = absorb_remote(state, below, row_start - distance * tok_dev)
        state = absorb_remote(state, above, row_start + distance * tok_dev)
    row_top, totals, summed = state
    attended = (
        jnp.transpose(summed / totals, (1, 0, 2)).reshape(tok_dev, local_width).astype(jnp.bfloat16)
    )
    tp_index = lax.axis_index("tp")
    quarter = tok_dev // 4
    partial_out = jnp.dot(attended, w_out, preferred_element_type=jnp.float32)
    full_out = lax.psum(partial_out.astype(jnp.bfloat16), "tp").astype(jnp.float32)
    residual = tokens.astype(jnp.float32) + full_out + b_out
    own_rows = lax.dynamic_index_in_dim(
        residual.reshape(quarter, 4, model_width), tp_index, 1, keepdims=False
    )
    merged_rows = layer_norm(own_rows, merge_gain, merge_bias).astype(jnp.bfloat16)
    owner_rows = owners[:, 0]
    capacity = max(2, 2 * quarter // seq_count)
    owner_table = (owner_rows[:, None] == jnp.arange(seq_count, dtype=jnp.int32)[None, :]).astype(
        jnp.int32
    )
    earlier = jnp.cumsum(owner_table, axis=0) - owner_table
    row_slot = jnp.sum(earlier * owner_table, axis=1)
    target_row = owner_rows * capacity + row_slot
    placing = (
        jnp.arange(seq_count * capacity, dtype=jnp.int32)[:, None] == target_row[None, :]
    ).astype(jnp.bfloat16)
    outgoing = jnp.dot(placing, merged_rows, preferred_element_type=jnp.float32).astype(
        jnp.bfloat16
    )
    return lax.all_to_all(outgoing, "seq", split_axis=0, concat_axis=0, tiled=True)


def solution(mesh):
    placed = (
        P("seq", None),
        P(),
        P(),
        P(None, None, "tp"),
        P(None, "tp"),
        P("tp", None),
        P(),
        P(),
        P(),
        P(),
        P("seq", None),
    )
    return jax.shard_map(
        per_device, mesh=mesh, in_specs=placed, out_specs=P("seq", "tp"), check_vma=False
    )
```

profile of v0, /device:TPU:32, one launch (start us, length us, event | category | flops | bytes accessed | tf_op | source)
XLA Modules:
  0.0 208.1 jit_solution(2838358114084987411)
XLA Ops:
  6.6 1.4 convert_reduce_fusion
  8.0 1.4 fusion.11
  9.4 1.7 fusion.36
  11.1 1.7 fusion.37
  12.8 1.9 collective-permute-start.1
  14.8 2.4 %collective-permute-start = (bf16[256,640]{0,1:T(8,128)(2,1)S(1)}, bf16[256,640]{0,1:T(8,128)(2,1)S(1)}, u32[]{:S(2)}, u32[]{:S(2)}) collective-permute-start(bf16[256,640]{0,1:T(8,128)(2,1)S(1)} %pad_maximum_fusion), channel_id=1, source_target_pairs={{0,4},{4,8},{8,12},{12,16},{16,20},{20,24},{24,28},{28,32},{32,36}... | collective-permute-start | bytes 983048 | tf_op jit(solution)/shard_map/ppermute | solution.py:15
  17.2 1.7 fusion.35
  18.9 5.0 %broadcast_in_dim.133 = s32[8192,4]{1,0:T(8,128)} broadcast(s32[8192]{0:T(1024)S(1)} %copy-done.2), dimensions={0} | broadcast | bytes 163840 | tf_op jit(solution)/shard_map/broadcast_in_dim | solution.py:48
  23.9 4.9 %reshape.637 = s32[32768]{0:T(1024)S(1)} reshape(s32[8192,4]{1,0:T(8,128)} %broadcast_in_dim.133) | data formatting | bytes 262144 | tf_op jit(solution)/shard_map/reshape | solution.py:48
  29.9 7.0 %collective-permute-start.3 = (bf16[256,640]{0,1:T(8,128)(2,1)S(1)}, bf16[256,640]{0,1:T(8,128)(2,1)S(1)}, u32[]{:S(2)}, u32[]{:S(2)}) collective-permute-start(bf16[256,640]{0,1:T(8,128)(2,1)S(1)} %collective-permute-done.1), channel_id=1, source_target_pairs={{4,0},{8,4},{12,8},{16,12},{20,16},{24,20},{28,24},{32,28},{36,32}... | collective-permute-start | bytes 983048 | tf_op jit(solution)/shard_map/ppermute | solution.py:15
  37.3 1.9 collective-permute-start.2
  39.6 6.1 %collective-permute-done.2 = bf16[256,640]{0,1:T(8,128)(2,1)S(1)} collective-permute-done((bf16[256,640]{0,1:T(8,128)(2,1)S(1)}, bf16[256,640]{0,1:T(8,128)(2,1)S(1)}, u32[]{:S(2)}, u32[]{:S(2)}) %collective-permute-start.2) | collective-permute-done | bytes 327712 | tf_op jit(solution)/shard_map/ppermute | solution.py:15
  45.7 1.9 collective-permute-start.4
  48.4 3.6 %collective-permute-start.5 = (bf16[256,640]{0,1:T(8,128)(2,1)S(1)}, bf16[256,640]{0,1:T(8,128)(2,1)S(1)}, u32[]{:S(2)}, u32[]{:S(2)}) collective-permute-start(bf16[256,640]{0,1:T(8,128)(2,1)S(1)} %collective-permute-done.3), channel_id=1, source_target_pairs={{4,0},{8,4},{12,8},{16,12},{20,16},{24,20},{28,24},{32,28},{36,32}... | collective-permute-start | bytes 983048 | tf_op jit(solution)/shard_map/ppermute | solution.py:15
  52.1 2.0 collective-permute-done.4
  54.1 1.9 collective-permute-start.6
  56.7 4.0 %collective-permute-start.7 = (bf16[256,640]{0,1:T(8,128)(2,1)S(1)}, bf16[256,640]{0,1:T(8,128)(2,1)S(1)}, u32[]{:S(2)}, u32[]{:S(2)}) collective-permute-start(bf16[256,640]{0,1:T(8,128)(2,1)S(1)} %collective-permute-done.5), channel_id=1, source_target_pairs={{4,0},{8,4},{12,8},{16,12},{20,16},{24,20},{28,24},{32,28},{36,32}... | collective-permute-start | bytes 983048 | tf_op jit(solution)/shard_map/ppermute | solution.py:15
  61.1 1.4 collective-permute-done.6
  62.9 2.1 %collective-permute-done.7 = bf16[256,640]{0,1:T(8,128)(2,1)S(1)} collective-permute-done((bf16[256,640]{0,1:T(8,128)(2,1)S(1)}, bf16[256,640]{0,1:T(8,128)(2,1)S(1)}, u32[]{:S(2)}, u32[]{:S(2)}) %collective-permute-start.7) | collective-permute-done | bytes 327712 | tf_op jit(solution)/shard_map/ppermute | solution.py:15
  69.7 1.4 convolution_convert_fusion.1
  71.5 66.9 %all-reduce.2.cloned.1.call-done = bf16[256,1280]{1,0:T(8,128)(2,1)} async-done(((bf16[256,1280]{1,0:T(8,128)(2,1)}), bf16[256,1280]{1,0:T(8,128)(2,1)}) %all-reduce.2.cloned.1.call-update) | async-done | bytes 655376 | tf_op jit(solution)/shard_map/psum | solution.py:106
  139.8 1.4 reshape.657
  141.2 1.9 fusion.102
  144.0 56.2 %all_to_all.12 = bf16[128,2,1280]{2,1,0:T(2,128)(2,1)S(1)} all-to-all(bf16[128,2,1280]{2,1,0:T(2,128)(2,1)S(1)} %all_to_all.8), channel_id=1, replica_groups=mesh['seq'=128,'tp'=4] {'seq'}, dimensions={0} | all-to-all | bytes 1310720 | tf_op jit(solution)/shard_map/all_to_all | solution.py:126
  (80 shorter events, 12.4 us)
Async XLA Ops:
  6.5 63.2 %copy-start = (bf16[320,1280]{1,0:T(8,128)(2,1)S(1)}, bf16[320,1280]{1,0:T(8,128)(2,1)}, u32[]{:S(2)}) copy-start(bf16[320,1280]{1,0:T(8,128)(2,1)} %param.16) | copy-start | bytes 2457604
  6.5 2.9 %copy-start.1 = (bf16[256,1280]{1,0:T(8,128)(2,1)S(1)}, bf16[256,1280]{1,0:T(8,128)(2,1)}, u32[]{:S(2)}) copy-start(bf16[256,1280]{1,0:T(8,128)(2,1)} %param.11) | copy-start | bytes 1966084
  6.5 2.8 %copy-start.6 = (f32[3,320]{1,0:T(4,128)S(1)}, f32[3,320]{1,0:T(4,128)}, u32[]{:S(2)}) copy-start(f32[3,320]{1,0:T(4,128)} %param.15) | copy-start | bytes 11524
  6.5 2.9 %copy-start.8 = (f32[1280]{0:T(1024)S(1)}, f32[1280]{0:T(1024)}, u32[]{:S(2)}) copy-start(f32[1280]{0:T(1024)} %param.13) | copy-start | bytes 15364
  6.5 2.9 %copy-start.9 = (f32[1280]{0:T(1024)S(1)}, f32[1280]{0:T(1024)}, u32[]{:S(2)}) copy-start(f32[1280]{0:T(1024)} %param.12) | copy-start | bytes 15364
  6.5 131.9 %all-reduce.2.cloned.1.call-start = ((), (), s32[]{:S(2)}) async-start(), calls=%async_computation.1 | async-start | bytes 1310720 | tf_op jit(solution)/shard_map/psum | solution.py:106
  12.8 17.0 %collective-permute-start.1 = (bf16[256,640]{0,1:T(8,128)(2,1)S(1)}, bf16[256,640]{0,1:T(8,128)(2,1)S(1)}, u32[]{:S(2)}, u32[]{:S(2)}) collective-permute-start(bf16[256,640]{0,1:T(8,128)(2,1)S(1)} %pad_maximum_fusion), channel_id=1, source_target_pairs={{4,0},{8,4},{12,8},{16,12},{20,16},{24,20},{28,24},{32,28},{36,32}... | collective-permute-start | bytes 983048 | tf_op jit(solution)/shard_map/ppermute | solution.py:15
  14.8 22.5 %collective-permute-start = (bf16[256,640]{0,1:T(8,128)(2,1)S(1)}, bf16[256,640]{0,1:T(8,128)(2,1)S(1)}, u32[]{:S(2)}, u32[]{:S(2)}) collective-permute-start(bf16[256,640]{0,1:T(8,128)(2,1)S(1)} %pad_maximum_fusion), channel_id=1, source_target_pairs={{0,4},{4,8},{8,12},{12,16},{16,20},{20,24},{24,28},{28,32},{32,36}... | collective-permute-start | bytes 983048 | tf_op jit(solution)/shard_map/ppermute | solution.py:15
  17.2 1.7 copy-start.2
  29.9 18.1 %collective-permute-start.3 = (bf16[256,640]{0,1:T(8,128)(2,1)S(1)}, bf16[256,640]{0,1:T(8,128)(2,1)S(1)}, u32[]{:S(2)}, u32[]{:S(2)}) collective-permute-start(bf16[256,640]{0,1:T(8,128)(2,1)S(1)} %collective-permute-done.1), channel_id=1, source_target_pairs={{4,0},{8,4},{12,8},{16,12},{20,16},{24,20},{28,24},{32,28},{36,32}... | collective-permute-start | bytes 983048 | tf_op jit(solution)/shard_map/ppermute | solution.py:15
  37.3 8.4 %collective-permute-start.2 = (bf16[256,640]{0,1:T(8,128)(2,1)S(1)}, bf16[256,640]{0,1:T(8,128)(2,1)S(1)}, u32[]{:S(2)}, u32[]{:S(2)}) collective-permute-start(bf16[256,640]{0,1:T(8,128)(2,1)S(1)} %collective-permute-done), channel_id=1, source_target_pairs={{0,4},{4,8},{8,12},{12,16},{16,20},{20,24},{24,28},{28,32},{32,36}... | collective-permute-start | bytes 983048 | tf_op jit(solution)/shard_map/ppermute | solution.py:15
  45.7 8.4 %collective-permute-start.4 = (bf16[256,640]{0,1:T(8,128)(2,1)S(1)}, bf16[256,640]{0,1:T(8,128)(2,1)S(1)}, u32[]{:S(2)}, u32[]{:S(2)}) collective-permute-start(bf16[256,640]{0,1:T(8,128)(2,1)S(1)} %collective-permute-done.2), channel_id=1, source_target_pairs={{0,4},{4,8},{8,12},{12,16},{16,20},{20,24},{24,28},{28,32},{32,36}... | collective-permute-start | bytes 983048 | tf_op jit(solution)/shard_map/ppermute | solution.py:15
  48.4 8.2 %collective-permute-start.5 = (bf16[256,640]{0,1:T(8,128)(2,1)S(1)}, bf16[256,640]{0,1:T(8,128)(2,1)S(1)}, u32[]{:S(2)}, u32[]{:S(2)}) collective-permute-start(bf16[256,640]{0,1:T(8,128)(2,1)S(1)} %collective-permute-done.3), channel_id=1, source_target_pairs={{4,0},{8,4},{12,8},{16,12},{20,16},{24,20},{28,24},{32,28},{36,32}... | collective-permute-start | bytes 983048 | tf_op jit(solution)/shard_map/ppermute | solution.py:15
  54.1 8.4 %collective-permute-start.6 = (bf16[256,640]{0,1:T(8,128)(2,1)S(1)}, bf16[256,640]{0,1:T(8,128)(2,1)S(1)}, u32[]{:S(2)}, u32[]{:S(2)}) collective-permute-start(bf16[256,640]{0,1:T(8,128)(2,1)S(1)} %collective-permute-done.4), channel_id=1, source_target_pairs={{0,4},{4,8},{8,12},{12,16},{16,20},{20,24},{24,28},{28,32},{32,36}... | collective-permute-start | bytes 983048 | tf_op jit(solution)/shard_map/ppermute | solution.py:15
  56.7 8.4 %collective-permute-start.7 = (bf16[256,640]{0,1:T(8,128)(2,1)S(1)}, bf16[256,640]{0,1:T(8,128)(2,1)S(1)}, u32[]{:S(2)}, u32[]{:S(2)}) collective-permute-start(bf16[256,640]{0,1:T(8,128)(2,1)S(1)} %collective-permute-done.5), channel_id=1, source_target_pairs={{4,0},{8,4},{12,8},{16,12},{20,16},{24,20},{28,24},{32,28},{36,32}... | collective-permute-start | bytes 983048 | tf_op jit(solution)/shard_map/ppermute | solution.py:15
  69.7 1.4 copy-start.7
  69.7 68.7 %copy-start.3 = (f32[1280]{0:T(1024)S(1)}, f32[1280]{0:T(1024)}, u32[]{:S(2)}) copy-start(f32[1280]{0:T(1024)} %param.17) | copy-start | bytes 15364
  139.7 3.6 %copy-start.4 = (f32[1280]{0:T(1024)S(1)}, f32[1280]{0:T(1024)}, u32[]{:S(2)}) copy-start(f32[1280]{0:T(1024)} %param.19) | copy-start | bytes 15364
  139.7 3.6 %copy-start.5 = (f32[1280]{0:T(1024)S(1)}, f32[1280]{0:T(1024)}, u32[]{:S(2)}) copy-start(f32[1280]{0:T(1024)} %param.18) | copy-start | bytes 15364
Sparse Core Ops, SparseCore 0:
  71.3 67.1 all-reduce.1
where the time goes:
time: 209 us; the launch traced here: 208 us
  waiting for transfers between devices  78.8 us (38%)
  blocking collectives  56.2 us (27%)
  starting transfers between devices  24.8 us (12%)
  between operations  13.8 us (7%)
  local copies, waits for them, and re-layouts  13.1 us (6%)
  matrix products  13 us (6%)
  other arithmetic  8.5 us (4%)
    psum x1, waiting for transfers between devices, per_device(): lax.psum(partial_out.astype(jnp.bfloat16), 'tp').astype(jnp.float32)  66.9 us
    all_to_all x1, blocking collectives, per_device(): lax.all_to_all(outgoing, 'seq', split_axis=0, concat_axis=0, tiled=True)  56.2 us
    ppermute x8, starting transfers between devices, from_behind(): lax.ppermute(value, axis, [(source, source + steps) for source in range(l...  24.7 us
    ppermute x8, waiting for transfers between devices, from_behind(): lax.ppermute(value, axis, [(source, source + steps) for source in range(l...  11.9 us
    broadcast_in_dim x1, local copies, waits for them, and re-layouts, per_device(): token_segment = jnp.repeat(segments, 4)  5.02 us
    reshape x1, local copies, waits for them, and re-layouts, per_device(): token_segment = jnp.repeat(segments, 4)  4.85 us
  transfers between devices with their start and end apart: 9, of which 6 were waited for; matrix products, arithmetic and copies ran while one was open for 8% of the time, Pallas kernels for 0%

commit v1 on v0

--- a/solution.py
+++ b/solution.py
@@ -103,7 +103,9 @@
     tp_index = lax.axis_index("tp")
     quarter = tok_dev // 4
     partial_out = jnp.dot(attended, w_out, preferred_element_type=jnp.float32)
-    full_out = lax.psum(partial_out.astype(jnp.bfloat16), "tp").astype(jnp.float32)
+    full_out = jnp.sum(lax.all_gather(partial_out.astype(jnp.bfloat16), "tp"), axis=0).astype(
+        jnp.float32
+    )
     residual = tokens.astype(jnp.float32) + full_out + b_out
     own_rows = lax.dynamic_index_in_dim(
         residual.reshape(quarter, 4, model_width), tp_index, 1, keepdims=False

time: 209 us -> 194 us (0.928)
  waiting for transfers between devices: 78.8 us -> 62.3 us
    psum x1 -> x0, waiting for transfers between devices: 66.9 us -> none  [per_device(): lax.psum(partial_out.astype(jnp.bfloat16), 'tp').astype(jnp.float32)]
    all_gather x0 -> x1, waiting for transfers between devices: none -> 50.5 us  [per_device(): lax.all_gather(partial_out.astype(jnp.bfloat16), 'tp')]
    reduce_sum x0 -> x1, other arithmetic: none -> 2.45 us  [per_device(): jnp.sum(lax.all_gather(partial_out.astype(jnp.bfloat16), 'tp'), axis=0)]
where the time goes in v1:
time: 194 us; the launch traced here: 193 us
  waiting for transfers between devices  62.3 us (32%)
  blocking collectives  56.2 us (29%)
  starting transfers between devices  24.8 us (13%)
  between operations  13.8 us (7%)
  local copies, waits for them, and re-layouts  13.1 us (7%)
  matrix products  13 us (7%)
  other arithmetic  9.87 us (5%)
    all_to_all x1, blocking collectives, per_device(): lax.all_to_all(outgoing, 'seq', split_axis=0, concat_axis=0, tiled=True)  56.2 us
    all_gather x1, waiting for transfers between devices, per_device(): lax.all_gather(partial_out.astype(jnp.bfloat16), 'tp')  50.5 us
    ppermute x8, starting transfers between devices, from_behind(): lax.ppermute(value, axis, [(source, source + steps) for source in range(l...  24.7 us
    ppermute x8, waiting for transfers between devices, from_behind(): lax.ppermute(value, axis, [(source, source + steps) for source in range(l...  11.9 us
    broadcast_in_dim x1, local copies, waits for them, and re-layouts, per_device(): token_segment = jnp.repeat(segments, 4)  5.02 us
    reshape x1, local copies, waits for them, and re-layouts, per_device(): token_segment = jnp.repeat(segments, 4)  4.85 us
  transfers between devices with their start and end apart: 9, of which 6 were waited for; matrix products, arithmetic and copies ran while one was open for 8% of the time, Pallas kernels for 0%

profile of v1, /device:TPU:32, one launch (start us, length us, event | category | flops | bytes accessed | tf_op | source)
XLA Modules:
  0.0 193.0 jit_solution(15886602226737197335)
XLA Ops:
  8.0 1.4 fusion.11
  9.4 1.7 fusion.36
  11.1 1.7 fusion.37
  12.8 1.9 collective-permute-start.1
  14.8 2.4 %collective-permute-start = (bf16[256,640]{0,1:T(8,128)(2,1)S(1)}, bf16[256,640]{0,1:T(8,128)(2,1)S(1)}, u32[]{:S(2)}, u32[]{:S(2)}) collective-permute-start(bf16[256,640]{0,1:T(8,128)(2,1)S(1)} %pad_maximum_fusion), channel_id=1, source_target_pairs={{0,4},{4,8},{8,12},{12,16},{16,20},{20,24},{24,28},{28,32},{32,36}... | collective-permute-start | bytes 983048 | tf_op jit(solution)/shard_map/ppermute | solution.py:15
  17.2 1.7 fusion.35
  18.9 5.0 %broadcast_in_dim.133 = s32[8192,4]{1,0:T(8,128)} broadcast(s32[8192]{0:T(1024)S(1)} %copy-done.2), dimensions={0} | broadcast | bytes 163840 | tf_op jit(solution)/shard_map/broadcast_in_dim | solution.py:48
  23.9 4.9 %reshape.637 = s32[32768]{0:T(1024)S(1)} reshape(s32[8192,4]{1,0:T(8,128)} %broadcast_in_dim.133) | data formatting | bytes 262144 | tf_op jit(solution)/shard_map/reshape | solution.py:48
  29.9 7.0 %collective-permute-start.3 = (bf16[256,640]{0,1:T(8,128)(2,1)S(1)}, bf16[256,640]{0,1:T(8,128)(2,1)S(1)}, u32[]{:S(2)}, u32[]{:S(2)}) collective-permute-start(bf16[256,640]{0,1:T(8,128)(2,1)S(1)} %collective-permute-done.1), channel_id=1, source_target_pairs={{4,0},{8,4},{12,8},{16,12},{20,16},{24,20},{28,24},{32,28},{36,32}... | collective-permute-start | bytes 983048 | tf_op jit(solution)/shard_map/ppermute | solution.py:15
  37.3 1.9 collective-permute-start.2
  39.6 6.1 %collective-permute-done.2 = bf16[256,640]{0,1:T(8,128)(2,1)S(1)} collective-permute-done((bf16[256,640]{0,1:T(8,128)(2,1)S(1)}, bf16[256,640]{0,1:T(8,128)(2,1)S(1)}, u32[]{:S(2)}, u32[]{:S(2)}) %collective-permute-start.2) | collective-permute-done | bytes 327712 | tf_op jit(solution)/shard_map/ppermute | solution.py:15
  45.7 1.9 collective-permute-start.4
  48.4 3.6 %collective-permute-start.5 = (bf16[256,640]{0,1:T(8,128)(2,1)S(1)}, bf16[256,640]{0,1:T(8,128)(2,1)S(1)}, u32[]{:S(2)}, u32[]{:S(2)}) collective-permute-start(bf16[256,640]{0,1:T(8,128)(2,1)S(1)} %collective-permute-done.3), channel_id=1, source_target_pairs={{4,0},{8,4},{12,8},{16,12},{20,16},{24,20},{28,24},{32,28},{36,32}... | collective-permute-start | bytes 983048 | tf_op jit(solution)/shard_map/ppermute | solution.py:15
  52.1 2.0 %collective-permute-done.4 = bf16[256,640]{0,1:T(8,128)(2,1)S(1)} collective-permute-done((bf16[256,640]{0,1:T(8,128)(2,1)S(1)}, bf16[256,640]{0,1:T(8,128)(2,1)S(1)}, u32[]{:S(2)}, u32[]{:S(2)}) %collective-permute-start.4) | collective-permute-done | bytes 327712 | tf_op jit(solution)/shard_map/ppermute | solution.py:15
  54.1 1.9 collective-permute-start.6
  56.7 4.0 %collective-permute-start.7 = (bf16[256,640]{0,1:T(8,128)(2,1)S(1)}, bf16[256,640]{0,1:T(8,128)(2,1)S(1)}, u32[]{:S(2)}, u32[]{:S(2)}) collective-permute-start(bf16[256,640]{0,1:T(8,128)(2,1)S(1)} %collective-permute-done.5), channel_id=1, source_target_pairs={{4,0},{8,4},{12,8},{16,12},{20,16},{24,20},{28,24},{32,28},{36,32}... | collective-permute-start | bytes 983048 | tf_op jit(solution)/shard_map/ppermute | solution.py:15
  61.1 1.4 collective-permute-done.6
  62.9 2.1 %collective-permute-done.7 = bf16[256,640]{0,1:T(8,128)(2,1)S(1)} collective-permute-done((bf16[256,640]{0,1:T(8,128)(2,1)S(1)}, bf16[256,640]{0,1:T(8,128)(2,1)S(1)}, u32[]{:S(2)}, u32[]{:S(2)}) %collective-permute-start.7) | collective-permute-done | bytes 327712 | tf_op jit(solution)/shard_map/ppermute | solution.py:15
  69.7 1.4 convolution_convert_fusion.1
  71.5 50.5 %all-gather.3.cloned.1.call-done = bf16[1024,1280]{1,0:T(8,128)(2,1)} async-done(((bf16[256,1280]{1,0:T(8,128)(2,1)}), bf16[1024,1280]{1,0:T(8,128)(2,1)}) %all-gather.3.cloned.1.call-update) | async-done | bytes 2621456 | tf_op jit(solution)/shard_map/all_gather | solution.py:106
  122.0 2.4 %reduce_sum.177 = bf16[256,1280]{1,0:T(8,128)(2,1)S(1)} reduce(bf16[4,256,1280]{2,1,0:T(8,128)(2,1)} %bitcast.272, bf16[]{:T(256)} %constant.90.clone.1), dimensions={0}, to_apply=%region_22.23 | reduce | flops 983040 | bytes 3276802 | tf_op jit(solution)/shard_map/reduce_sum | solution.py:106
  124.6 1.4 reshape.657
  126.1 1.9 fusion.102
  128.9 56.2 %all_to_all.12 = bf16[128,2,1280]{2,1,0:T(2,128)(2,1)S(1)} all-to-all(bf16[128,2,1280]{2,1,0:T(2,128)(2,1)S(1)} %all_to_all.8), channel_id=1, replica_groups=mesh['seq'=128,'tp'=4] {'seq'}, dimensions={0} | all-to-all | bytes 1310720 | tf_op jit(solution)/shard_map/all_to_all | solution.py:128
  (81 shorter events, 12.7 us)
Async XLA Ops:
  6.5 63.2 %copy-start = (bf16[320,1280]{1,0:T(8,128)(2,1)S(1)}, bf16[320,1280]{1,0:T(8,128)(2,1)}, u32[]{:S(2)}) copy-start(bf16[320,1280]{1,0:T(8,128)(2,1)} %param.16) | copy-start | bytes 2457604
  6.5 2.9 %copy-start.1 = (bf16[256,1280]{1,0:T(8,128)(2,1)S(1)}, bf16[256,1280]{1,0:T(8,128)(2,1)}, u32[]{:S(2)}) copy-start(bf16[256,1280]{1,0:T(8,128)(2,1)} %param.11) | copy-start | bytes 1966084
  6.5 2.8 %copy-start.6 = (f32[3,320]{1,0:T(4,128)S(1)}, f32[3,320]{1,0:T(4,128)}, u32[]{:S(2)}) copy-start(f32[3,320]{1,0:T(4,128)} %param.15) | copy-start | bytes 11524
  6.5 2.9 %copy-start.8 = (f32[1280]{0:T(1024)S(1)}, f32[1280]{0:T(1024)}, u32[]{:S(2)}) copy-start(f32[1280]{0:T(1024)} %param.13) | copy-start | bytes 15364
  6.5 2.9 %copy-start.9 = (f32[1280]{0:T(1024)S(1)}, f32[1280]{0:T(1024)}, u32[]{:S(2)}) copy-start(f32[1280]{0:T(1024)} %param.12) | copy-start | bytes 15364
  6.5 115.4 %all-gather.3.cloned.1.call-start = ((), (), s32[]{:S(2)}) async-start(), calls=%async_computation.1 | async-start | bytes 3276800 | tf_op jit(solution)/shard_map/all_gather | solution.py:106
  12.8 17.0 %collective-permute-start.1 = (bf16[256,640]{0,1:T(8,128)(2,1)S(1)}, bf16[256,640]{0,1:T(8,128)(2,1)S(1)}, u32[]{:S(2)}, u32[]{:S(2)}) collective-permute-start(bf16[256,640]{0,1:T(8,128)(2,1)S(1)} %pad_maximum_fusion), channel_id=1, source_target_pairs={{4,0},{8,4},{12,8},{16,12},{20,16},{24,20},{28,24},{32,28},{36,32}... | collective-permute-start | bytes 983048 | tf_op jit(solution)/shard_map/ppermute | solution.py:15
  14.8 22.5 %collective-permute-start = (bf16[256,640]{0,1:T(8,128)(2,1)S(1)}, bf16[256,640]{0,1:T(8,128)(2,1)S(1)}, u32[]{:S(2)}, u32[]{:S(2)}) collective-permute-start(bf16[256,640]{0,1:T(8,128)(2,1)S(1)} %pad_maximum_fusion), channel_id=1, source_target_pairs={{0,4},{4,8},{8,12},{12,16},{16,20},{20,24},{24,28},{28,32},{32,36}... | collective-permute-start | bytes 983048 | tf_op jit(solution)/shard_map/ppermute | solution.py:15
  17.2 1.7 copy-start.2
  29.9 18.1 %collective-permute-start.3 = (bf16[256,640]{0,1:T(8,128)(2,1)S(1)}, bf16[256,640]{0,1:T(8,128)(2,1)S(1)}, u32[]{:S(2)}, u32[]{:S(2)}) collective-permute-start(bf16[256,640]{0,1:T(8,128)(2,1)S(1)} %collective-permute-done.1), channel_id=1, source_target_pairs={{4,0},{8,4},{12,8},{16,12},{20,16},{24,20},{28,24},{32,28},{36,32}... | collective-permute-start | bytes 983048 | tf_op jit(solution)/shard_map/ppermute | solution.py:15
  37.3 8.4 %collective-permute-start.2 = (bf16[256,640]{0,1:T(8,128)(2,1)S(1)}, bf16[256,640]{0,1:T(8,128)(2,1)S(1)}, u32[]{:S(2)}, u32[]{:S(2)}) collective-permute-start(bf16[256,640]{0,1:T(8,128)(2,1)S(1)} %collective-permute-done), channel_id=1, source_target_pairs={{0,4},{4,8},{8,12},{12,16},{16,20},{20,24},{24,28},{28,32},{32,36}... | collective-permute-start | bytes 983048 | tf_op jit(solution)/shard_map/ppermute | solution.py:15
  45.7 8.4 %collective-permute-start.4 = (bf16[256,640]{0,1:T(8,128)(2,1)S(1)}, bf16[256,640]{0,1:T(8,128)(2,1)S(1)}, u32[]{:S(2)}, u32[]{:S(2)}) collective-permute-start(bf16[256,640]{0,1:T(8,128)(2,1)S(1)} %collective-permute-done.2), channel_id=1, source_target_pairs={{0,4},{4,8},{8,12},{12,16},{16,20},{20,24},{24,28},{28,32},{32,36}... | collective-permute-start | bytes 983048 | tf_op jit(solution)/shard_map/ppermute | solution.py:15
  48.4 8.2 %collective-permute-start.5 = (bf16[256,640]{0,1:T(8,128)(2,1)S(1)}, bf16[256,640]{0,1:T(8,128)(2,1)S(1)}, u32[]{:S(2)}, u32[]{:S(2)}) collective-permute-start(bf16[256,640]{0,1:T(8,128)(2,1)S(1)} %collective-permute-done.3), channel_id=1, source_target_pairs={{4,0},{8,4},{12,8},{16,12},{20,16},{24,20},{28,24},{32,28},{36,32}... | collective-permute-start | bytes 983048 | tf_op jit(solution)/shard_map/ppermute | solution.py:15
  54.1 8.4 %collective-permute-start.6 = (bf16[256,640]{0,1:T(8,128)(2,1)S(1)}, bf16[256,640]{0,1:T(8,128)(2,1)S(1)}, u32[]{:S(2)}, u32[]{:S(2)}) collective-permute-start(bf16[256,640]{0,1:T(8,128)(2,1)S(1)} %collective-permute-done.4), channel_id=1, source_target_pairs={{0,4},{4,8},{8,12},{12,16},{16,20},{20,24},{24,28},{28,32},{32,36}... | collective-permute-start | bytes 983048 | tf_op jit(solution)/shard_map/ppermute | solution.py:15
  56.7 8.4 %collective-permute-start.7 = (bf16[256,640]{0,1:T(8,128)(2,1)S(1)}, bf16[256,640]{0,1:T(8,128)(2,1)S(1)}, u32[]{:S(2)}, u32[]{:S(2)}) collective-permute-start(bf16[256,640]{0,1:T(8,128)(2,1)S(1)} %collective-permute-done.5), channel_id=1, source_target_pairs={{4,0},{8,4},{12,8},{16,12},{20,16},{24,20},{28,24},{32,28},{36,32}... | collective-permute-start | bytes 983048 | tf_op jit(solution)/shard_map/ppermute | solution.py:15
  69.7 1.4 copy-start.7
  122.0 2.5 %copy-start.3 = (f32[1280]{0:T(1024)S(1)}, f32[1280]{0:T(1024)}, u32[]{:S(2)}) copy-start(f32[1280]{0:T(1024)} %param.17) | copy-start | bytes 15364
  124.6 3.6 %copy-start.4 = (f32[1280]{0:T(1024)S(1)}, f32[1280]{0:T(1024)}, u32[]{:S(2)}) copy-start(f32[1280]{0:T(1024)} %param.19) | copy-start | bytes 15364
  124.6 3.6 %copy-start.5 = (f32[1280]{0:T(1024)S(1)}, f32[1280]{0:T(1024)}, u32[]{:S(2)}) copy-start(f32[1280]{0:T(1024)} %param.18) | copy-start | bytes 15364
Sparse Core Ops, SparseCore 0:
  71.3 50.6 all-gather.2
